TPU v7x, 512 devices: a whole 4x4x16 slice. The times are simulated.
512 devices in a mesh: dp: 16 (over z), expert: 32 (over y, x, core).
Axes of the slice: x: 4, y: 4, z: 16, core: 2. Of those that a mesh axis runs over, the one named last changes fastest.
Arguments:
- tokens: bfloat16 [65536, 1024], P(('dp', 'expert')), may hold values from -24 to 24
- expert_ids: int32 [65536, 2], P(('dp', 'expert')), may hold values from 0 to 31, all different within a row; in each aligned block of 128 rows (0 to 127, 128 to 255, ...) at most 32 rows name the same one
- route_probs: float32 [65536, 2], P(('dp', 'expert')), may hold values from 0.1 to 1
- w_gate: bfloat16 [32, 1024, 384], P('expert', 'dp'), may hold values from -0.1875 to 0.1875
- w_up: bfloat16 [32, 1024, 384], P('expert', 'dp'), may hold values from -0.1875 to 0.1875
- w_down: bfloat16 [32, 384, 1024], P('expert', None, 'dp'), may hold values from -0.3125 to 0.3125
- grad_out: bfloat16 [65536, 1024], P(('dp', 'expert')), may hold values from -2.5 to 2.5
Outputs:
- mixed_out: bfloat16 [65536, 1024], P(('dp', 'expert'))
- grad_tokens: bfloat16 [65536, 1024], P(('dp', 'expert'))
- grad_probs: float32 [65536, 2], P(('dp', 'expert'))
- grad_w_gate: bfloat16 [32, 1024, 384], P('expert', 'dp')
- grad_w_up: bfloat16 [32, 1024, 384], P('expert', 'dp')
- grad_w_down: bfloat16 [32, 384, 1024], P('expert', None, 'dp')
Inputs may be any that keep to these rules, and one draw needn't show every extreme that they name: `expert_ids`: each row names 2 different experts. Within the rows of one device no expert is named by more than 32 rows, and in every draw some expert is named by exactly 32 rows of some device.
All inputs are finite; a program needn't handle non-finite values.
Results may differ from a plain program's by a relative error of at most 0.017.
Values may be sent and summed in bfloat16 or wider, within the bound.
No kernel may reach another device: no remote copies, remote signals or barrier semaphores. Data moves between devices by JAX's collectives and lax.ppermute only.
A program may use at most 128 MiB of HBM per device.

v0:
```python
import jax
import jax.numpy as jnp
from jax import lax
from jax.sharding import PartitionSpec as P


def route_slots(expert_ids, experts):
    flat_ids = expert_ids.reshape(-1)
    onehot = (flat_ids[:, None] == jnp.arange(experts, dtype=jnp.int32)[None, :]).astype(jnp.int32)
    before = jnp.cumsum(onehot, axis=0) - onehot
    slot_of = jnp.sum(before * onehot, axis=1)
    return (flat_ids, slot_of, jnp.sum(onehot, axis=0))


def contract_rows(left_op, right_op):
    return lax.dot_general(
        left_op, right_op, (((0,), (0,)), ((), ())), preferred_element_type=jnp.float32
    )


def contract_cols(left_op, right_op):
    return lax.dot_general(
        left_op, right_op, (((1,), (1,)), ((), ())), preferred_element_type=jnp.float32
    )


def forward_whole(slot_rows, gate_full, up_full, down_full):
    gate_pre = jnp.dot(slot_rows, gate_full, preferred_element_type=jnp.float32)
    up_pre = jnp.dot(slot_rows, up_full, preferred_element_type=jnp.float32)
    hidden = (gate_pre * jax.nn.sigmoid(gate_pre) * up_pre).astype(jnp.bfloat16)
    expert_out = jnp.dot(hidden, down_full, preferred_element_type=jnp.float32).astype(jnp.bfloat16)
    return (gate_pre, up_pre, hidden, expert_out)


def backward_whole(slot_rows, stored, grad_in, gate_full, up_full, down_full):
    gate_pre, up_pre, hidden, expert_out = stored
    back_hidden = contract_cols(grad_in, down_full)
    sigmoid_g = jax.nn.sigmoid(gate_pre)
    activated = gate_pre * sigmoid_g
    back_gate = (back_hidden * up_pre * sigmoid_g * (1.0 + gate_pre * (1.0 - sigmoid_g))).astype(
        jnp.bfloat16
    )
    back_up = (back_hidden * activated).astype(jnp.bfloat16)
    back_rows = (contract_cols(back_gate, gate_full) + contract_cols(back_up, up_full)).astype(
        jnp.bfloat16
    )
    return (
        back_rows,
        contract_rows(slot_rows, back_gate),
        contract_rows(slot_rows, back_up),
        contract_rows(hidden, grad_in),
    )


def shards(tokens, expert_ids, route_probs, w_gate, w_up, w_down, grad_out):
    senders = lax.axis_size("expert")
    tok_rows, model_width = tokens.shape
    top_count = expert_ids.shape[1]
    capacity = min(tok_rows, 4 * tok_rows * top_count // senders)
    total_rows = senders * capacity
    flat_ids, slot_of, local_counts = route_slots(expert_ids, senders)
    slot_place = flat_ids * capacity + slot_of
    token_of = jnp.arange(tok_rows * top_count, dtype=jnp.int32) // top_count
    outgoing = (
        jnp.zeros((total_rows, model_width), jnp.bfloat16).at[slot_place].set(tokens[token_of])
    )
    gathered = (
        lax.all_gather(w_gate, "dp", axis=1, tiled=True),
        lax.all_gather(w_up, "dp", axis=1, tiled=True),
        lax.all_gather(w_down, "dp", axis=2, tiled=True),
    )
    gate_full, up_full, down_full = (gathered[0][0], gathered[1][0], gathered[2][0])
    arrived = lax.all_to_all(
        outgoing.reshape(senders, capacity, model_width),
        "expert",
        split_axis=0,
        concat_axis=0,
        tiled=True,
    )
    slot_rows = arrived.reshape(total_rows, model_width)
    stored = forward_whole(slot_rows, gate_full, up_full, down_full)
    returned = lax.all_to_all(
        stored[3].reshape(senders, capacity, model_width),
        "expert",
        split_axis=0,
        concat_axis=0,
        tiled=True,
    )
    picked = (
        returned.reshape(total_rows, model_width)[slot_place]
        .reshape(tok_rows, top_count, model_width)
        .astype(jnp.float32)
    )
    mixed_out = jnp.sum(route_probs[:, :, None] * picked, axis=1).astype(jnp.bfloat16)
    grad_wide = grad_out.astype(jnp.float32)
    grad_probs = jnp.sum(grad_wide[:, None, :] * picked, axis=2)
    scaled = (
        (route_probs[:, :, None] * grad_wide[:, None, :])
        .astype(jnp.bfloat16)
        .reshape(tok_rows * top_count, model_width)
    )
    grad_send = jnp.zeros((total_rows, model_width), jnp.bfloat16).at[slot_place].set(scaled)
    grad_in = lax.all_to_all(
        grad_send.reshape(senders, capacity, model_width),
        "expert",
        split_axis=0,
        concat_axis=0,
        tiled=True,
    ).reshape(total_rows, model_width)
    back_rows, grad_gate, grad_up, grad_down = backward_whole(
        slot_rows, stored, grad_in, gate_full, up_full, down_full
    )
    sent_back = lax.all_to_all(
        back_rows.reshape(senders, capacity, model_width),
        "expert",
        split_axis=0,
        concat_axis=0,
        tiled=True,
    )
    back_picked = sent_back.reshape(total_rows, model_width)[slot_place].reshape(
        tok_rows, top_count, model_width
    )
    grad_tokens = jnp.sum(back_picked.astype(jnp.float32), axis=1).astype(jnp.bfloat16)
    shares = (
        lax.psum_scatter(
            grad_gate[None].astype(jnp.bfloat16), "dp", scatter_dimension=1, tiled=True
        ).astype(jnp.float32),
        lax.psum_scatter(
            grad_up[None].astype(jnp.bfloat16), "dp", scatter_dimension=1, tiled=True
        ).astype(jnp.float32),
        lax.psum_scatter(
            grad_down[None].astype(jnp.bfloat16), "dp", scatter_dimension=2, tiled=True
        ).astype(jnp.float32),
    )
    return (
        mixed_out,
        grad_tokens,
        grad_probs,
        shares[0].astype(jnp.bfloat16),
        shares[1].astype(jnp.bfloat16),
        shares[2].astype(jnp.bfloat16),
    )


def solution(mesh):
    placed = (
        P(("dp", "expert"), None),
        P(("dp", "expert"), None),
        P(("dp", "expert"), None),
        P("expert", "dp", None),
        P("expert", "dp", None),
        P("expert", None, "dp"),
        P(("dp", "expert"), None),
    )
    return jax.shard_map(
        shards,
        mesh=mesh,
        in_specs=placed,
        out_specs=(
            P(("dp", "expert"), None),
            P(("dp", "expert"), None),
            P(("dp", "expert"), None),
            P("expert", "dp", None),
            P("expert", "dp", None),
            P("expert", None, "dp"),
        ),
        check_vma=False,
    )
```

profile of v0, /device:TPU:4, one launch (start us, length us, event | category | flops | bytes accessed | tf_op | source)
XLA Modules:
  0.0 398.8 jit_solution(18079659399550357771)
XLA Ops:
  10.2 5.0 %scatter_custom_fusion = bf16[1024,1024]{1,0:T(8,128)(2,1)} fusion(s32[256]{0:T(256)S(1)} %bitcast.81, bf16[]{:T(256)} %constant.26.clone.1, bf16[128,1024]{1,0:T(8,128)(2,1)S(1)} %copy-done, s32[1024]{0:T(1024)S(1)} %pad_clamp_fusion.1), kind=kCustom, calls=%fused_computation.23 | custom fusion | bytes 2097154 | tf_op jit(solution)/shard_map/scatter | solution.py:65
  15.2 10.4 %all-to-all-start = ((bf16[32,32,1024]{2,1,0:T(8,128)(2,1)}), bf16[32,32,1024]{2,1,0:T(8,128)(2,1)}, u32[]{:S(2)}, u32[]{:S(2)}) async-start(bf16[32,32,1024]{2,1,0:T(8,128)(2,1)} %bitcast.4), calls=%async_computation | async-start | bytes 4194304 | tf_op jit(solution)/shard_map/all_to_all | solution.py:73
  26.9 3.3 scatter_custom_fusion.1
  30.2 22.1 %all-to-all-done = bf16[32,32,1024]{2,1,0:T(8,128)(2,1)} async-done(((bf16[32,32,1024]{2,1,0:T(8,128)(2,1)}), bf16[32,32,1024]{2,1,0:T(8,128)(2,1)}, u32[]{:S(2)}, u32[]{:S(2)}) %all-to-all-start) | async-done | bytes 2097184 | tf_op jit(solution)/shard_map/all_to_all | solution.py:73
  52.3 7.5 %all-to-all-start.2 = ((bf16[32,32,1024]{2,1,0:T(8,128)(2,1)}), bf16[32,32,1024]{2,1,0:T(8,128)(2,1)S(1)}, u32[]{:S(2)}, u32[]{:S(2)}) async-start(bf16[32,32,1024]{2,1,0:T(8,128)(2,1)} %bitcast.76), calls=%async_computation.2 | async-start | bytes 4194304 | tf_op jit(solution)/shard_map/all_to_all | solution.py:103
  59.8 37.7 %all_gather.9 = bf16[1,1024,384]{2,1,0:T(8,128)(2,1)S(1)} all-gather(bf16[1,64,384]{2,1,0:T(8,128)(2,1)S(1)} %copy-done.7), channel_id=1, replica_groups=mesh['dp'=16,'expert'=32] {'dp'}, dimensions={1}, use_global_device_ids=true | all-gather | bytes 835584 | tf_op jit(solution)/shard_map/all_gather | solution.py:68
  97.6 31.0 %all_gather.10 = bf16[1,1024,384]{2,1,0:T(8,128)(2,1)S(1)} all-gather(bf16[1,64,384]{2,1,0:T(8,128)(2,1)} %param.11), channel_id=1, replica_groups=mesh['dp'=16,'expert'=32] {'dp'}, dimensions={1}, use_global_device_ids=true | all-gather | bytes 835584 | tf_op jit(solution)/shard_map/all_gather | solution.py:69
  128.6 35.5 %all_gather.11 = bf16[1,384,1024]{1,2,0:T(8,128)(2,1)} all-gather(bf16[1,384,64]{1,2,0:T(8,128)(2,1)} %param.12), channel_id=1, replica_groups=mesh['dp'=16,'expert'=32] {'dp'}, dimensions={2}, use_global_device_ids=true | all-gather | bytes 835584 | tf_op jit(solution)/shard_map/all_gather | solution.py:70
  164.0 4.1 %fusion.12 = f32[1024,384]{1,0:T(8,128)} fusion(bf16[1024,1024]{1,0:T(8,128)(2,1)} %bitcast.5, bf16[1,1024,384]{2,1,0:T(8,128)(2,1)S(1)} %all_gather.10), kind=kOutput, calls=%fused_computation.30 | convolution fusion | flops 805306368 | bytes 4456448 | tf_op jit(solution)/shard_map/dot_general | solution.py:29
  168.1 4.0 fusion.16
  172.1 5.1 %multiply_convert_fusion = (bf16[1024,384]{1,0:T(8,128)(2,1)}, bf16[1024,384]{1,0:T(8,128)(2,1)}, bf16[1024,384]{1,0:T(8,128)(2,1)S(1)}) fusion(f32[1024,384]{1,0:T(8,128)} %fusion.16, f32[1024,384]{1,0:T(8,128)} %fusion.12, bf16[1024,1024]{1,0:T(8,128)(2,1)S(1)} %bitcast.74, bf16[1,384,1024]{1,2,0:T(8,128)(2,1)} %all_gather.11), kind=kOutput, calls=%fused_computation.7 | convolution fusion | flops 811204608 | bytes 8388608 | tf_op jit(solution)/shard_map/dot_general | solution.py:22
  180.0 4.1 %copy.30 = bf16[1,384,1024]{1,0,2:T(2,128)(2,1)S(1)} copy(bf16[1,384,1024]{2,1,0:T(8,128)(2,1)} %fusion.3) | data formatting | bytes 1572864
  185.2 4.0 %convolution_convert_fusion = bf16[1024,1024]{1,0:T(8,128)(2,1)} fusion(bf16[1024,384]{1,0:T(8,128)(2,1)} %copy-done.4, bf16[1,384,1024]{1,2,0:T(8,128)(2,1)} %all_gather.11), kind=kOutput, calls=%fused_computation.6 | convolution fusion | flops 806354944 | bytes 3670016 | tf_op jit(solution)/shard_map/dot_general | solution.py:31
  189.2 7.4 %all-to-all-start.1 = ((bf16[32,32,1024]{2,1,0:T(8,128)(2,1)}), bf16[32,32,1024]{2,1,0:T(8,128)(2,1)S(1)}, u32[]{:S(2)}, u32[]{:S(2)}) async-start(bf16[32,32,1024]{2,1,0:T(8,128)(2,1)} %bitcast.80), calls=%async_computation.1 | async-start | bytes 4194304 | tf_op jit(solution)/shard_map/all_to_all | solution.py:82
  196.7 4.0 fusion.1
  203.2 2.6 add_convert_fusion
  205.9 17.3 %all-to-all-done.1 = bf16[32,32,1024]{2,1,0:T(8,128)(2,1)S(1)} async-done(((bf16[32,32,1024]{2,1,0:T(8,128)(2,1)}), bf16[32,32,1024]{2,1,0:T(8,128)(2,1)S(1)}, u32[]{:S(2)}, u32[]{:S(2)}) %all-to-all-start.1) | async-done | bytes 2097184 | tf_op jit(solution)/shard_map/all_to_all | solution.py:82
  223.1 8.2 %all-to-all-start.3 = ((bf16[32,32,1024]{2,1,0:T(8,128)(2,1)}), bf16[32,32,1024]{2,1,0:T(8,128)(2,1)}, u32[]{:S(2)}, u32[]{:S(2)}) async-start(bf16[32,32,1024]{2,1,0:T(8,128)(2,1)} %bitcast.77), calls=%async_computation.3 | async-start | bytes 4194304 | tf_op jit(solution)/shard_map/all_to_all | solution.py:113
  231.6 3.8 fusion.2
  236.3 13.9 %reduce-scatter.10.cloned.1.call-done = bf16[64,384]{1,0:T(8,128)(2,1)} async-done(((bf16[1024,384]{1,0:T(8,128)(2,1)}), bf16[64,384]{1,0:T(8,128)(2,1)}) %reduce-scatter.10.cloned.1.call-update) | async-done | bytes 49168
  255.3 3.6 multiply_reduce_fusion
  259.6 3.4 gather_fusion.1
  265.3 56.1 %reduce-scatter.6.cloned.1.call-done = bf16[1,64,384]{2,1,0:T(8,128)(2,1)} async-done(((bf16[1,1024,384]{2,1,0:T(8,128)(2,1)}), bf16[1,64,384]{2,1,0:T(8,128)(2,1)}) %reduce-scatter.6.cloned.1.call-update) | async-done | bytes 49168 | tf_op jit(solution)/shard_map/reduce_scatter | solution.py:125
  321.4 70.9 %reduce-scatter.8.cloned.1.call-done = bf16[1,64,384]{2,1,0:T(8,128)(2,1)} async-done(((bf16[1,1024,384]{2,1,0:T(8,128)(2,1)}), bf16[1,64,384]{2,1,0:T(8,128)(2,1)}) %reduce-scatter.8.cloned.1.call-update) | async-done | bytes 49168 | tf_op jit(solution)/shard_map/reduce_scatter | solution.py:128
  (57 shorter events, 19.9 us)
Async XLA Ops:
  7.2 3.0 copy-start
  15.2 10.4 %copy-start.8 = (f32[128,2]{0,1:T(2,128)S(1)}, f32[128,2]{0,1:T(2,128)}, u32[]{:S(2)}) copy-start(f32[128,2]{0,1:T(2,128)} %param.9) | copy-start | bytes 3076
  15.2 10.7 %copy-start.3 = (bf16[128,1024]{1,0:T(8,128)(2,1)S(1)}, bf16[128,1024]{1,0:T(8,128)(2,1)}, u32[]{:S(2)}) copy-start(bf16[128,1024]{1,0:T(8,128)(2,1)} %param.13) | copy-start | bytes 786436
  15.2 37.0 %all-to-all-start = ((bf16[32,32,1024]{2,1,0:T(8,128)(2,1)}), bf16[32,32,1024]{2,1,0:T(8,128)(2,1)}, u32[]{:S(2)}, u32[]{:S(2)}) async-start(bf16[32,32,1024]{2,1,0:T(8,128)(2,1)} %bitcast.4), calls=%async_computation | async-start | bytes 4194304 | tf_op jit(solution)/shard_map/all_to_all | solution.py:73
  52.3 7.6 %copy-start.7 = (bf16[1,64,384]{2,1,0:T(8,128)(2,1)S(1)}, bf16[1,64,384]{2,1,0:T(8,128)(2,1)}, u32[]{:S(2)}) copy-start(bf16[1,64,384]{2,1,0:T(8,128)(2,1)} %param.10) | copy-start | bytes 147460
  52.3 119.8 %all-to-all-start.2 = ((bf16[32,32,1024]{2,1,0:T(8,128)(2,1)}), bf16[32,32,1024]{2,1,0:T(8,128)(2,1)S(1)}, u32[]{:S(2)}, u32[]{:S(2)}) async-start(bf16[32,32,1024]{2,1,0:T(8,128)(2,1)} %bitcast.76), calls=%async_computation.2 | async-start | bytes 4194304 | tf_op jit(solution)/shard_map/all_to_all | solution.py:103
  59.8 190.4 %reduce-scatter.10.cloned.1.call-start = ((), (), s32[]{:S(2)}) async-start(), calls=%async_computation.9 | async-start | bytes 835584
  128.6 39.5 %copy-start.1 = (bf16[1,1024,384]{2,1,0:T(8,128)(2,1)}, bf16[1,1024,384]{2,1,0:T(8,128)(2,1)S(1)}, u32[]{:S(2)}) copy-start(bf16[1,1024,384]{2,1,0:T(8,128)(2,1)S(1)} %all_gather.10) | copy-start | bytes 2359300
  177.2 0.9 copy-start.4
  189.2 33.9 %all-to-all-start.1 = ((bf16[32,32,1024]{2,1,0:T(8,128)(2,1)}), bf16[32,32,1024]{2,1,0:T(8,128)(2,1)S(1)}, u32[]{:S(2)}, u32[]{:S(2)}) async-start(bf16[32,32,1024]{2,1,0:T(8,128)(2,1)} %bitcast.80), calls=%async_computation.1 | async-start | bytes 4194304 | tf_op jit(solution)/shard_map/all_to_all | solution.py:82
  196.6 124.8 %reduce-scatter.6.cloned.1.call-start = ((), (), s32[]{:S(2)}) async-start(), calls=%async_computation.7 | async-start | bytes 835584 | tf_op jit(solution)/shard_map/reduce_scatter | solution.py:125
  200.6 2.6 copy-start.2
  200.6 2.6 copy-start.5
  223.1 8.5 %copy-start.6 = (bf16[1024,384]{1,0:T(8,128)(2,1)S(1)}, bf16[1024,384]{1,0:T(8,128)(2,1)}, u32[]{:S(2)}) copy-start(bf16[1024,384]{1,0:T(8,128)(2,1)} %get-tuple-element.26) | copy-start | bytes 2359300
  223.1 36.4 %all-to-all-start.3 = ((bf16[32,32,1024]{2,1,0:T(8,128)(2,1)}), bf16[32,32,1024]{2,1,0:T(8,128)(2,1)}, u32[]{:S(2)}, u32[]{:S(2)}) async-start(bf16[32,32,1024]{2,1,0:T(8,128)(2,1)} %bitcast.77), calls=%async_computation.3 | async-start | bytes 4194304 | tf_op jit(solution)/shard_map/all_to_all | solution.py:113
  231.3 161.0 %reduce-scatter.8.cloned.1.call-start = ((), (), s32[]{:S(2)}) async-start(), calls=%async_computation.8 | async-start | bytes 835584 | tf_op jit(solution)/shard_map/reduce_scatter | solution.py:128
Sparse Core Ops, SparseCore 0:
  185.3 64.8 reduce-scatter.9
  253.8 67.5 reduce-scatter.5
  324.8 67.4 reduce-scatter.7
where the time goes:
time: 400 us; the launch traced here: 399 us
  waiting for transfers between devices  180 us (45%)
  blocking collectives  104 us (26%)
  starting transfers between devices  33.8 us (8%)
  matrix products  32 us (8%)
  local copies, waits for them, and re-layouts  23.2 us (6%)
  between operations  14 us (4%)
  other arithmetic  11.4 us (3%)
    reduce_scatter x1, waiting for transfers between devices, shards(): lax.psum_scatter(grad_up[None].astype(jnp.bfloat16), 'dp', scatter_dimens...  70.9 us
    reduce_scatter x1, waiting for transfers between devices, shards(): lax.psum_scatter(grad_gate[None].astype(jnp.bfloat16), 'dp', scatter_dime...  56.1 us
    all_gather x1, blocking collectives, shards(): lax.all_gather(w_gate, 'dp', axis=1, tiled=True)  37.7 us
    all_gather x1, blocking collectives, shards(): lax.all_gather(w_down, 'dp', axis=2, tiled=True)  35.5 us
    all_gather x1, blocking collectives, shards(): lax.all_gather(w_up, 'dp', axis=1, tiled=True)  31 us
    all_to_all x1, waiting for transfers between devices, shards(): lax.all_to_all(outgoing.reshape(senders, capacity, model_width), 'expert'...  22.1 us
    all_to_all x1, waiting for transfers between devices, shards(): lax.all_to_all(stored[3].reshape(senders, capacity, model_width), 'expert...  17.3 us
    unnamed x4, waiting for transfers between devices  13.9 us
  transfers between devices with their start and end apart: 7, of which 5 were waited for; matrix products, arithmetic and copies ran while one was open for 11% of the time, Pallas kernels for 0%

commit v1 on v0

--- a/solution.py
+++ b/solution.py
@@ -67,7 +67,9 @@
     gathered = (
         lax.all_gather(w_gate, "dp", axis=1, tiled=True),
         lax.all_gather(w_up, "dp", axis=1, tiled=True),
-        lax.all_gather(w_down, "dp", axis=2, tiled=True),
+        jnp.concatenate(
+            lax.all_to_all(jnp.stack([w_down] * lax.axis_size("dp")), "dp", 0, 0), axis=2
+        ),
     )
     gate_full, up_full, down_full = (gathered[0][0], gathered[1][0], gathered[2][0])
     arrived = lax.all_to_all(

time: 400 us -> 435 us (1.087)
  the two profiles are of different devices: /device:TPU:4 before, /device:TPU:6 now
where the time goes in v1:
time: 435 us; the launch traced here: 434 us
  waiting for transfers between devices  180 us (41%)
  blocking collectives  134 us (31%)
  starting transfers between devices  37.4 us (9%)
  matrix products  30.7 us (7%)
  local copies, waits for them, and re-layouts  26.2 us (6%)
  between operations  14 us (3%)
  other arithmetic  11.3 us (3%)
    reduce_scatter x1, waiting for transfers between devices, shards(): lax.psum_scatter(grad_up[None].astype(jnp.bfloat16), 'dp', scatter_dimens...  71.2 us
    all_gather x1, blocking collectives, shards(): lax.all_gather(w_gate, 'dp', axis=1, tiled=True)  66.1 us
    reduce_scatter x1, waiting for transfers between devices, shards(): lax.psum_scatter(grad_gate[None].astype(jnp.bfloat16), 'dp', scatter_dime...  56.1 us
    all_to_all x1, blocking collectives, shards(): lax.all_to_all(outgoing.reshape(senders, capacity, model_width), 'expert'...  35.2 us
    all_gather x1, blocking collectives, shards(): lax.all_gather(w_up, 'dp', axis=1, tiled=True)  32.9 us
    all_to_all x1, waiting for transfers between devices, shards(): lax.all_to_all(grad_send.reshape(senders, capacity, model_width), 'expert...  20.6 us
    all_to_all x1, waiting for transfers between devices, shards(): lax.all_to_all(stored[3].reshape(senders, capacity, model_width), 'expert...  16.3 us
    unnamed x4, waiting for transfers between devices  16.1 us
  transfers between devices with their start and end apart: 7, of which 5 were waited for; matrix products, arithmetic and copies ran while one was open for 10% of the time, Pallas kernels for 0%

profile of v1, /device:TPU:6, one launch (start us, length us, event | category | flops | bytes accessed | tf_op | source)
XLA Modules:
  0.0 433.9 jit_solution(10455446144635310351)
XLA Ops:
  13.1 3.3 scatter_custom_fusion.1
  16.4 9.5 %all-to-all-start.3 = ((bf16[32,32,1024]{2,1,0:T(8,128)(2,1)}), bf16[32,32,1024]{2,1,0:T(8,128)(2,1)S(1)}, u32[]{:S(2)}, u32[]{:S(2)}) async-start(bf16[32,32,1024]{2,1,0:T(8,128)(2,1)} %bitcast.77), calls=%async_computation.3 | async-start | bytes 4194304 | tf_op jit(solution)/shard_map/all_to_all | solution.py:105
  26.0 5.0 %scatter_custom_fusion = bf16[1024,1024]{1,0:T(8,128)(2,1)} fusion(s32[256]{0:T(256)S(1)} %bitcast.89, bf16[]{:T(256)} %constant.26.clone.1, bf16[128,1024]{1,0:T(8,128)(2,1)S(1)} %copy-done, s32[1024]{0:T(1024)S(1)} %pad_clamp_fusion.1), kind=kCustom, calls=%fused_computation.23 | custom fusion | bytes 2097154 | tf_op jit(solution)/shard_map/scatter | solution.py:65
  31.0 20.6 %all-to-all-done.3 = bf16[32,32,1024]{2,1,0:T(8,128)(2,1)S(1)} async-done(((bf16[32,32,1024]{2,1,0:T(8,128)(2,1)}), bf16[32,32,1024]{2,1,0:T(8,128)(2,1)S(1)}, u32[]{:S(2)}, u32[]{:S(2)}) %all-to-all-start.3) | async-done | bytes 2097184 | tf_op jit(solution)/shard_map/all_to_all | solution.py:105
  51.6 35.2 %all_to_all.25 = bf16[32,32,1024]{2,1,0:T(8,128)(2,1)} all-to-all(bf16[32,32,1024]{2,1,0:T(8,128)(2,1)} %bitcast.78), channel_id=1, replica_groups=mesh['dp'=16,'expert'=32] {'expert'}, dimensions={0} | all-to-all | bytes 4194304 | tf_op jit(solution)/shard_map/all_to_all | solution.py:75
  87.8 13.2 %all-to-all-start.1 = ((bf16[16,1,384,64]{2,3,1,0:T(8,128)(2,1)}), bf16[16,1,384,64]{2,3,1,0:T(8,128)(2,1)}, u32[]{:S(2)}, u32[]{:S(2)}) async-start(bf16[16,1,384,64]{2,3,1,0:T(8,128)(2,1)} %stack.2), calls=%async_computation.1 | async-start | bytes 1572864 | tf_op jit(solution)/shard_map/all_to_all | solution.py:71
  101.0 66.1 %all_gather.6 = bf16[1,1024,384]{2,1,0:T(8,128)(2,1)S(1)} all-gather(bf16[1,64,384]{2,1,0:T(8,128)(2,1)S(1)} %copy-done.9), channel_id=1, replica_groups=mesh['dp'=16,'expert'=32] {'dp'}, dimensions={1}, use_global_device_ids=true | all-gather | bytes 835584 | tf_op jit(solution)/shard_map/all_gather | solution.py:68
  167.1 32.9 %all_gather.7 = bf16[1,1024,384]{2,1,0:T(8,128)(2,1)S(1)} all-gather(bf16[1,64,384]{2,1,0:T(8,128)(2,1)S(1)} %copy-done.10), channel_id=1, replica_groups=mesh['dp'=16,'expert'=32] {'dp'}, dimensions={1}, use_global_device_ids=true | all-gather | bytes 835584 | tf_op jit(solution)/shard_map/all_gather | solution.py:69
  200.0 4.4 %fusion.9 = f32[1024,384]{1,0:T(8,128)} fusion(bf16[1024,1024]{1,0:T(8,128)(2,1)} %bitcast.82, bf16[1,1024,384]{2,1,0:T(8,128)(2,1)S(1)} %all_gather.7), kind=kOutput, calls=%fused_computation.27 | convolution fusion | flops 805306368 | bytes 4456448 | tf_op jit(solution)/shard_map/dot_general | solution.py:29
  206.8 5.1 %multiply_convert_fusion = (bf16[1024,384]{1,0:T(8,128)(2,1)}, bf16[1024,384]{1,0:T(8,128)(2,1)}, bf16[1024,384]{1,0:T(8,128)(2,1)S(1)}) fusion(f32[1024,384]{1,0:T(8,128)} %fusion.13, f32[1024,384]{1,0:T(8,128)} %fusion.9, bf16[1024,1024]{1,0:T(8,128)(2,1)S(1)} %bitcast.75, bf16[384,1024]{0,1:T(8,128)(2,1)} %bitcast.11), kind=kOutput, calls=%fused_computation.7 | convolution fusion | flops 811204608 | bytes 8388608 | tf_op jit(solution)/shard_map/dot_general | solution.py:22
  214.7 4.1 copy.32
  220.2 3.8 convolution_convert_fusion
  224.0 5.3 %all-to-all-start.2 = ((bf16[32,32,1024]{2,1,0:T(8,128)(2,1)}), bf16[32,32,1024]{2,1,0:T(8,128)(2,1)S(1)}, u32[]{:S(2)}, u32[]{:S(2)}) async-start(bf16[32,32,1024]{2,1,0:T(8,128)(2,1)} %bitcast.86), calls=%async_computation.2 | async-start | bytes 4194304 | tf_op jit(solution)/shard_map/all_to_all | solution.py:84
  229.3 3.9 fusion.1
  233.3 2.5 fusion.11
  235.8 2.6 add_convert_fusion
  238.5 16.3 %all-to-all-done.2 = bf16[32,32,1024]{2,1,0:T(8,128)(2,1)S(1)} async-done(((bf16[32,32,1024]{2,1,0:T(8,128)(2,1)}), bf16[32,32,1024]{2,1,0:T(8,128)(2,1)S(1)}, u32[]{:S(2)}, u32[]{:S(2)}) %all-to-all-start.2) | async-done | bytes 2097184 | tf_op jit(solution)/shard_map/all_to_all | solution.py:84
  254.8 9.0 %all-to-all-start.4 = ((bf16[32,32,1024]{2,1,0:T(8,128)(2,1)}), bf16[32,32,1024]{2,1,0:T(8,128)(2,1)}, u32[]{:S(2)}, u32[]{:S(2)}) async-start(bf16[32,32,1024]{2,1,0:T(8,128)(2,1)} %bitcast.79), calls=%async_computation.4 | async-start | bytes 4194304 | tf_op jit(solution)/shard_map/all_to_all | solution.py:115
  264.1 3.9 fusion.2
  269.0 16.0 %reduce-scatter.10.cloned.1.call-done = bf16[64,384]{1,0:T(8,128)(2,1)} async-done(((bf16[1024,384]{1,0:T(8,128)(2,1)}), bf16[64,384]{1,0:T(8,128)(2,1)}) %reduce-scatter.10.cloned.1.call-update) | async-done | bytes 49168
  290.2 3.6 multiply_reduce_fusion
  294.4 3.4 gather_fusion.1
  300.1 56.1 %reduce-scatter.6.cloned.1.call-done = bf16[1,64,384]{2,1,0:T(8,128)(2,1)} async-done(((bf16[1,1024,384]{2,1,0:T(8,128)(2,1)}), bf16[1,64,384]{2,1,0:T(8,128)(2,1)}) %reduce-scatter.6.cloned.1.call-update) | async-done | bytes 49168 | tf_op jit(solution)/shard_map/reduce_scatter | solution.py:127
  356.2 71.2 %reduce-scatter.8.cloned.1.call-done = bf16[1,64,384]{2,1,0:T(8,128)(2,1)} async-done(((bf16[1,1024,384]{2,1,0:T(8,128)(2,1)}), bf16[1,64,384]{2,1,0:T(8,128)(2,1)}) %reduce-scatter.8.cloned.1.call-update) | async-done | bytes 49168 | tf_op jit(solution)/shard_map/reduce_scatter | solution.py:130
  (62 shorter events, 22.8 us)
Async XLA Ops:
  7.2 18.8 %copy-start = (bf16[128,1024]{1,0:T(8,128)(2,1)S(1)}, bf16[128,1024]{1,0:T(8,128)(2,1)}, u32[]{:S(2)}) copy-start(bf16[128,1024]{1,0:T(8,128)(2,1)} %param.7) | copy-start | bytes 786436
  16.4 35.2 %all-to-all-start.3 = ((bf16[32,32,1024]{2,1,0:T(8,128)(2,1)}), bf16[32,32,1024]{2,1,0:T(8,128)(2,1)S(1)}, u32[]{:S(2)}, u32[]{:S(2)}) async-start(bf16[32,32,1024]{2,1,0:T(8,128)(2,1)} %bitcast.77), calls=%async_computation.3 | async-start | bytes 4194304 | tf_op jit(solution)/shard_map/all_to_all | solution.py:105
  51.6 35.2 %copy-start.8 = (bf16[1,384,64]{1,2,0:T(8,128)(2,1)S(1)}, bf16[1,384,64]{1,2,0:T(8,128)(2,1)}, u32[]{:S(2)}) copy-start(bf16[1,384,64]{1,2,0:T(8,128)(2,1)} %param.12) | copy-start | bytes 147460
  86.7 14.3 %copy-start.9 = (bf16[1,64,384]{2,1,0:T(8,128)(2,1)S(1)}, bf16[1,64,384]{2,1,0:T(8,128)(2,1)}, u32[]{:S(2)}) copy-start(bf16[1,64,384]{2,1,0:T(8,128)(2,1)} %param.10) | copy-start | bytes 147460
  86.7 80.3 %copy-start.10 = (bf16[1,64,384]{2,1,0:T(8,128)(2,1)S(1)}, bf16[1,64,384]{2,1,0:T(8,128)(2,1)}, u32[]{:S(2)}) copy-start(bf16[1,64,384]{2,1,0:T(8,128)(2,1)} %param.11) | copy-start | bytes 147460
  87.8 119.0 %all-to-all-start.1 = ((bf16[16,1,384,64]{2,3,1,0:T(8,128)(2,1)}), bf16[16,1,384,64]{2,3,1,0:T(8,128)(2,1)}, u32[]{:S(2)}, u32[]{:S(2)}) async-start(bf16[16,1,384,64]{2,3,1,0:T(8,128)(2,1)} %stack.2), calls=%async_computation.1 | async-start | bytes 1572864 | tf_op jit(solution)/shard_map/all_to_all | solution.py:71
  100.9 184.1 %reduce-scatter.10.cloned.1.call-start = ((), (), s32[]{:S(2)}) async-start(), calls=%async_computation.10 | async-start | bytes 835584
  200.0 4.4 %copy-start.1 = (bf16[1,1024,384]{2,1,0:T(8,128)(2,1)}, bf16[1,1024,384]{2,1,0:T(8,128)(2,1)S(1)}, u32[]{:S(2)}) copy-start(bf16[1,1024,384]{2,1,0:T(8,128)(2,1)S(1)} %all_gather.7) | copy-start | bytes 2359300
  200.0 4.4 %copy-start.3 = (bf16[32,32,1024]{2,1,0:T(8,128)(2,1)S(1)}, bf16[32,32,1024]{2,1,0:T(8,128)(2,1)}, u32[]{:S(2)}) copy-start(bf16[32,32,1024]{2,1,0:T(8,128)(2,1)} %all_to_all.25) | copy-start | bytes 6291460
  211.9 0.9 copy-start.5
  218.8 1.3 copy-start.6
  224.0 30.8 %all-to-all-start.2 = ((bf16[32,32,1024]{2,1,0:T(8,128)(2,1)}), bf16[32,32,1024]{2,1,0:T(8,128)(2,1)S(1)}, u32[]{:S(2)}, u32[]{:S(2)}) async-start(bf16[32,32,1024]{2,1,0:T(8,128)(2,1)} %bitcast.86), calls=%async_computation.2 | async-start | bytes 4194304 | tf_op jit(solution)/shard_map/all_to_all | solution.py:84
  229.3 127.0 %reduce-scatter.6.cloned.1.call-start = ((), (), s32[]{:S(2)}) async-start(), calls=%async_computation.8 | async-start | bytes 835584 | tf_op jit(solution)/shard_map/reduce_scatter | solution.py:127
  233.3 2.6 copy-start.2
  233.3 2.6 copy-start.7
  254.8 39.6 %all-to-all-start.4 = ((bf16[32,32,1024]{2,1,0:T(8,128)(2,1)}), bf16[32,32,1024]{2,1,0:T(8,128)(2,1)}, u32[]{:S(2)}, u32[]{:S(2)}) async-start(bf16[32,32,1024]{2,1,0:T(8,128)(2,1)} %bitcast.79), calls=%async_computation.4 | async-start | bytes 4194304 | tf_op jit(solution)/shard_map/all_to_all | solution.py:115
  263.9 4.2 copy-start.4
  263.9 163.5 %reduce-scatter.8.cloned.1.call-start = ((), (), s32[]{:S(2)}) async-start(), calls=%async_computation.9 | async-start | bytes 835584 | tf_op jit(solution)/shard_map/reduce_scatter | solution.py:130
Sparse Core Ops, SparseCore 0:
  220.0 64.9 reduce-scatter.9
  288.6 67.5 reduce-scatter.5
  359.6 67.7 reduce-scatter.7
